TPU v7x, 512 devices: a whole 4x8x8 slice. The times are simulated.
512 devices in a mesh: dp: 8 (over z), expert: 64 (over y, x, core).
Axes of the slice: x: 4, y: 8, z: 8, core: 2. Of those that a mesh axis runs over, the one named last changes fastest.
Arguments:
- query: bfloat16 [128, 8192], P('dp'), may hold values from -1200 to 1200
- new_kv: bfloat16 [128, 1024], P('dp'), may hold values from -5 to 5
- kv_cache: bfloat16 [128, 1024, 1024], P('dp', 'expert'), may hold values from -6 to 6
- lengths: int32 [128], P('dp'), may hold values from 2 to 1024, as said below
- fork_parent: int32 [64], replicated, may hold values from 0 to 127, as said below
- fork_child: int32 [64], replicated, may hold values from 0 to 126, as said below
- fork_block: int32 [64], replicated, may hold values from 0 to 63, as said below
- out_weight: bfloat16 [8192, 4096], P('expert'), may hold values from -1 to 1
- residual: bfloat16 [128, 4096], P('dp'), may hold values from -300 to 300
- route_ids: int32 [128, 8], replicated, may hold values from 0 to 63, all different within a row; in each aligned block of 16 rows (0 to 15, 16 to 31, ...) at most 4 rows name the same one
- route_weights: float32 [128, 8], replicated, may hold values from 0.02 to 0.3
- w_gate: bfloat16 [64, 4096, 1024], P('expert', None, 'dp'), may hold values from -0.09375 to 0.09375
- w_up: bfloat16 [64, 4096, 1024], P('expert', None, 'dp'), may hold values from -0.09375 to 0.09375
- w_down: bfloat16 [64, 1024, 4096], P('expert', 'dp'), may hold values from -0.1875 to 0.1875
Outputs:
- attn_proj: bfloat16 [128, 4096], P('dp', 'expert')
- expert_mix: bfloat16 [128, 4096], P('dp', 'expert')
Inputs may be any that keep to these rules, and one draw needn't show every extreme that they name: `lengths`: at least 2; a fork's child has its parent's length. `fork_parent`: fork g * 8 + d takes its parent from the branches g * 16 to (g + 1) * 16 - 1 and its child from d * 16 to (d + 1) * 16 - 1; parents are distinct, children are distinct, and no child is a parent. `fork_child`: see fork_parent. `fork_block`: at most the block that holds the parent's last cached position, (lengths - 1) // 16. `route_ids`: in each aligned block of 16 rows no expert is named by more than 4 rows, a bound that some block reaches.
All inputs are finite; a program needn't handle non-finite values.
Results may differ from a plain program's by a relative error of at most 0.024.
Values may be sent and summed in bfloat16 or wider, within the bound.
No kernel may reach another device: no remote copies, remote signals or barrier semaphores. Data moves between devices by JAX's collectives and lax.ppermute only.
A program may use at most 128 MiB of HBM per device.

v0:
```python
import math
import jax
import jax.numpy as jnp
from jax import lax
from jax.sharding import PartitionSpec as P

HD = 128
KVH = 4


def combined_all(array, axis, join):
    gathered = jax.tree.map(
        lambda a, kind: lax.all_gather(a.astype(kind), axis),
        array,
        (jnp.bfloat16, jnp.bfloat16, jnp.bfloat16),
    )

    def take(source):
        return jax.tree.map(
            lambda a, own: lax.dynamic_index_in_dim(a, source, 0, False).astype(own.dtype),
            gathered,
            array,
        )

    return lax.fori_loop(
        1, lax.axis_size(axis), lambda source, state: join(state, take(source)), take(0)
    )


def combine_parts(first, second):
    out_first, peak_first, sum_first = first
    out_second, peak_second, sum_second = second
    highest = jnp.maximum(peak_first, peak_second)
    factor_first = jnp.exp(peak_first - highest)
    factor_second = jnp.exp(peak_second - highest)
    merged_out = out_first * factor_first[..., None] + out_second * factor_second[..., None]
    return (merged_out, highest, sum_first * factor_first + sum_second * factor_second)


def shards(
    query,
    new_kv,
    kv_cache,
    lengths,
    fork_parent,
    fork_child,
    fork_block,
    out_weight,
    residual,
    route_ids,
    route_weights,
    w_gate,
    w_up,
    w_down,
):
    groups = lax.axis_size("dp")
    owners = lax.axis_size("expert")
    group_index = lax.axis_index("dp")
    owner_index = lax.axis_index("expert")
    local_rows = query.shape[0]
    positions_dev = kv_cache.shape[1]
    key_width = KVH * HD
    head_count = query.shape[1] // HD
    grouping = head_count // KVH
    own_heads = head_count // owners
    model_width = residual.shape[1]
    columns = model_width // owners
    outgoing = (
        lax.dynamic_slice_in_dim(fork_parent, group_index * groups, groups)
        - group_index * local_rows
    )
    out_blocks = lax.dynamic_slice_in_dim(fork_block, group_index * groups, groups)
    send_rows = jnp.where(
        (owner_index >= out_blocks)[:, None, None],
        kv_cache[outgoing],
        jnp.zeros((), kv_cache.dtype),
    )
    arrived = lax.all_to_all(send_rows, "dp", split_axis=0, concat_axis=0, tiled=True)
    incoming = jnp.arange(groups, dtype=jnp.int32) * groups + group_index
    targets = fork_child[incoming] - group_index * local_rows
    take_new = owner_index >= fork_block[incoming]
    cache = kv_cache.at[targets].set(jnp.where(take_new[:, None, None], arrived, kv_cache[targets]))
    score_scale = 1.0 / math.sqrt(HD)
    positions = owner_index * positions_dev + jnp.arange(positions_dev, dtype=jnp.int32)
    visible = positions[None, :] < lengths[:, None]
    cached_keys = cache[:, :, :key_width].reshape(local_rows, positions_dev, KVH, HD)
    cached_values = cache[:, :, key_width:].reshape(local_rows, positions_dev, KVH, HD)
    grouped = query.reshape(local_rows, KVH, grouping, HD)
    scores = (
        jnp.einsum("bkgd,bpkd->bkgp", grouped, cached_keys, preferred_element_type=jnp.float32)
        * score_scale
    )
    scores = jnp.where(visible[:, None, None, :], scores, -1e30)
    highest = jnp.max(scores, axis=3)
    weights = jnp.where(visible[:, None, None, :], jnp.exp(scores - highest[..., None]), 0.0)
    weight_sum = jnp.sum(weights, axis=3)
    partial_out = jnp.einsum(
        "bkgp,bpkd->bkgd",
        weights.astype(jnp.bfloat16),
        cached_values,
        preferred_element_type=jnp.float32,
    )
    partial_out = partial_out.reshape(local_rows, head_count, HD)
    highest = highest.reshape(local_rows, head_count)
    weight_sum = weight_sum.reshape(local_rows, head_count)
    merged = combined_all((partial_out, highest, weight_sum), "expert", combine_parts)
    head_out = lax.dynamic_slice_in_dim(merged[0], owner_index * own_heads, own_heads, 1)
    head_peak = lax.dynamic_slice_in_dim(merged[1], owner_index * own_heads, own_heads, 1)
    head_sum = lax.dynamic_slice_in_dim(merged[2], owner_index * own_heads, own_heads, 1)
    own_query = lax.dynamic_slice_in_dim(query, owner_index * own_heads * HD, own_heads * HD, 1)
    own_query = own_query.reshape(local_rows, own_heads, HD).astype(jnp.float32)
    kv_index = (owner_index * own_heads + jnp.arange(own_heads, dtype=jnp.int32)) // grouping
    new_keys = jnp.take(
        new_kv[:, :key_width].reshape(local_rows, KVH, HD), kv_index, axis=1
    ).astype(jnp.float32)
    new_values = jnp.take(
        new_kv[:, key_width:].reshape(local_rows, KVH, HD), kv_index, axis=1
    ).astype(jnp.float32)
    own_score = jnp.sum(own_query * new_keys, axis=2) * score_scale
    new_peak = jnp.maximum(head_peak, own_score)
    old_factor = jnp.exp(head_peak - new_peak)
    own_weight = jnp.exp(own_score - new_peak)
    denominator = head_sum * old_factor + own_weight
    own_rounded = lax.optimization_barrier(own_weight.astype(jnp.bfloat16)).astype(jnp.float32)
    attended = (
        head_out * old_factor[..., None] + own_rounded[..., None] * new_values
    ) / denominator[..., None]
    attended = attended.astype(jnp.bfloat16).reshape(local_rows, own_heads * HD)
    proj_terms = jnp.dot(attended, out_weight, preferred_element_type=jnp.float32)
    projected = lax.psum(proj_terms, "expert")
    stream = residual.astype(jnp.float32) + projected
    inverse = lax.rsqrt(jnp.sum(stream * stream, axis=1, keepdims=True) / model_width + 1e-06)
    normed = (stream * inverse).astype(jnp.bfloat16)
    attn_cols = lax.dynamic_slice_in_dim(projected, owner_index * columns, columns, 1).astype(
        jnp.bfloat16
    )
    top_k = route_ids.shape[1]
    experts_total = w_gate.shape[0] * owners
    capacity = max(2, 2 * local_rows * top_k // experts_total)
    own_ids = lax.dynamic_slice_in_dim(route_ids, group_index * local_rows, local_rows, 0)
    own_gates = lax.dynamic_slice_in_dim(route_weights, group_index * local_rows, local_rows, 0)
    matched = (own_ids == owner_index).astype(jnp.int32).reshape(-1)
    ranking = jnp.cumsum(matched) - 1
    slot_ids = jnp.arange(capacity, dtype=jnp.int32)
    onehot = ((matched[:, None] == 1) & (ranking[:, None] == slot_ids[None, :])).astype(jnp.float32)
    chosen = onehot.reshape(local_rows, top_k, capacity)
    dispatch = jnp.sum(chosen, axis=1).T
    slot_gate = jnp.sum(chosen * own_gates[:, :, None], axis=(0, 1))
    dispatch, slot_gate = (dispatch, slot_gate)
    routed = jnp.dot(
        dispatch.astype(jnp.bfloat16), normed, preferred_element_type=jnp.float32
    ).astype(jnp.bfloat16)
    piece = lax.all_gather(routed, "dp", axis=0, tiled=True)
    gate_proj = jnp.dot(piece, w_gate[0], preferred_element_type=jnp.float32)
    up_proj = jnp.dot(piece, w_up[0], preferred_element_type=jnp.float32)
    hidden = (jax.nn.silu(gate_proj) * up_proj).astype(jnp.bfloat16)
    outputs = jnp.dot(hidden, w_down[0], preferred_element_type=jnp.float32)
    summed = lax.psum_scatter(
        outputs.astype(jnp.bfloat16), "dp", scatter_dimension=0, tiled=True
    ).astype(jnp.float32)
    spread = jnp.dot(dispatch.T * slot_gate[None, :], summed, precision=lax.Precision.HIGHEST)
    mix_cols = lax.psum_scatter(spread, "expert", scatter_dimension=1, tiled=True).astype(
        jnp.bfloat16
    )
    return (attn_cols, mix_cols)


def solution(mesh):
    in_specs = (
        P("dp", None),
        P("dp", None),
        P("dp", "expert", None),
        P("dp"),
        P(),
        P(),
        P(),
        P("expert", None),
        P("dp", None),
        P(),
        P(),
        P("expert", None, "dp"),
        P("expert", None, "dp"),
        P("expert", "dp", None),
    )
    out_specs = (P("dp", "expert"), P("dp", "expert"))
    return jax.shard_map(shards, mesh=mesh, in_specs=in_specs, out_specs=out_specs, check_vma=False)
```

profile of v0, /device:TPU:16, one launch (start us, length us, event | category | flops | bytes accessed | tf_op | source)
XLA Modules:
  0.0 687.0 jit_solution(2898068980157066316)
XLA Ops:
  11.2 10.3 %all-to-all-start = ((bf16[8,16,1024]{2,1,0:T(8,128)(2,1)}), bf16[8,16,1024]{2,1,0:T(8,128)(2,1)S(1)}, u32[]{:S(2)}, u32[]{:S(2)}) async-start(bf16[8,16,1024]{2,1,0:T(8,128)(2,1)} %broadcast_select_fusion), calls=%async_computation | async-start | bytes 524288 | tf_op jit(solution)/shard_map/all_to_all | solution.py:78
  24.8 1.7 copy.82
  27.3 6.2 all-to-all-done
  40.0 39.2 %all_gather.17 = bf16[64,16,64]{2,1,0:T(8,128)(2,1)S(1)} all-gather(bf16[1,16,64]{2,1,0:T(8,128)(2,1)S(1)} %convert_element_type.161), channel_id=1, replica_groups=mesh['dp'=8,'expert'=64] {'expert'}, dimensions={0}, use_global_device_ids=true | all-gather | bytes 133120 | tf_op jit(solution)/shard_map/all_gather | solution.py:13
  79.3 37.2 %all_gather.16 = bf16[64,16,64]{2,1,0:T(8,128)(2,1)S(1)} all-gather(bf16[1,16,64]{2,1,0:T(8,128)(2,1)S(1)} %convert_element_type.157), channel_id=1, replica_groups=mesh['dp'=8,'expert'=64] {'expert'}, dimensions={0}, use_global_device_ids=true | all-gather | bytes 133120 | tf_op jit(solution)/shard_map/all_gather | solution.py:13
  116.5 21.4 %all-gather.3.cloned.1.call-done = bf16[64,16,64,128]{3,2,1,0:T(8,128)(2,1)} async-done(((bf16[1,16,64,128]{3,2,1,0:T(8,128)(2,1)}), bf16[64,16,64,128]{3,2,1,0:T(8,128)(2,1)}) %all-gather.3.cloned.1.call-update) | async-done | bytes 16777232 | tf_op jit(solution)/shard_map/all_gather | solution.py:13
  138.9 94.9 %while.20 = (s32[]{:T(128)}, f32[16,64,128]{2,1,0:T(8,128)S(1)}, f32[16,64]{1,0:T(8,128)S(1)}, f32[16,64]{1,0:T(8,128)S(1)}, bf16[64,16,64]{2,1,0:T(8,128)(2,1)S...) while((s32[]{:T(128)}, f32[16,64,128]{2,1,0:T(8,128)S(1)}, ...), condition=%wide.region_4.5_spmd, body=%wide.region_3.4_spmd.sunk | while | flops 532485 | bytes 1347735 | solution.py:25
  138.9 1.5 fusion.71
  140.4 1.5 fusion.71
  141.9 1.5 fusion.71
  145.0 1.5 fusion.71
  148.0 1.5 fusion.71
  151.0 1.5 fusion.71
  154.0 1.5 fusion.71
  157.0 1.5 fusion.71
  160.0 1.5 fusion.71
  163.0 1.5 fusion.71
  235.8 181.4 %all-reduce.4.cloned.1.call-done = f32[16,4096]{1,0:T(8,128)} async-done(((f32[16,4096]{1,0:T(8,128)}), f32[16,4096]{1,0:T(8,128)}) %all-reduce.4.cloned.1.call-update) | async-done | bytes 262160 | tf_op jit(solution)/shard_map/psum | solution.py:130
  419.4 26.8 %all-gather = bf16[8,4,4096]{2,1,0:T(4,128)(2,1)S(1)} all-gather(bf16[1,4,4096]{2,1,0:T(4,128)(2,1)S(1)} %fusion.3), channel_id=1, replica_groups=mesh['dp'=8,'expert'=64] {'dp'}, dimensions={0}, use_global_device_ids=true | all-gather | bytes 294912 | tf_op jit(solution)/shard_map/all_gather | solution.py:153
  446.3 1.5 fusion.10
  447.8 2.5 convolution_convert_fusion
  452.3 75.5 %all-reduce.6.cloned.1.call-done = bf16[32,4096]{1,0:T(8,128)(2,1)} async-done(((bf16[32,4096]{1,0:T(8,128)(2,1)}), bf16[32,4096]{1,0:T(8,128)(2,1)}) %all-reduce.6.cloned.1.call-update) | async-done | bytes 262160
  527.8 3.4 convolution_bitcast_fusion
  532.6 146.4 %reduce-scatter.4.cloned.1.call-done = f32[64,16]{1,0:T(8,128)} async-done(((f32[4096,16]{1,0:T(8,128)}), f32[64,16]{1,0:T(8,128)}) %reduce-scatter.4.cloned.1.call-update) | async-done | bytes 4112
  (188 shorter events, 102.2 us)
Async XLA Ops:
  7.2 440.7 %copy-start = (bf16[1,128,4096]{2,1,0:T(8,128)(2,1)S(1)}, bf16[1,128,4096]{2,1,0:T(8,128)(2,1)}, u32[]{:S(2)}) copy-start(bf16[1,128,4096]{2,1,0:T(8,128)(2,1)} %param.31) | copy-start | bytes 3145732
  7.2 227.1 %copy-start.1 = (bf16[128,4096]{1,0:T(8,128)(2,1)S(1)}, bf16[128,4096]{1,0:T(8,128)(2,1)}, u32[]{:S(2)}) copy-start(bf16[128,4096]{1,0:T(8,128)(2,1)} %param.25) | copy-start | bytes 3145732
  7.2 410.0 %copy-start.2 = (bf16[16,4096]{1,0:T(8,128)(2,1)S(1)}, bf16[16,4096]{1,0:T(8,128)(2,1)}, u32[]{:S(2)}) copy-start(bf16[16,4096]{1,0:T(8,128)(2,1)} %param.26) | copy-start | bytes 393220
  7.2 228.2 %copy-start.3 = (f32[128,8]{0,1:T(8,128)S(1)}, f32[128,8]{0,1:T(8,128)}, u32[]{:S(2)}) copy-start(f32[128,8]{0,1:T(8,128)} %param.28) | copy-start | bytes 12292
  11.2 22.2 %all-to-all-start = ((bf16[8,16,1024]{2,1,0:T(8,128)(2,1)}), bf16[8,16,1024]{2,1,0:T(8,128)(2,1)S(1)}, u32[]{:S(2)}, u32[]{:S(2)}) async-start(bf16[8,16,1024]{2,1,0:T(8,128)(2,1)} %broadcast_select_fusion), calls=%async_computation | async-start | bytes 524288 | tf_op jit(solution)/shard_map/all_to_all | solution.py:78
  21.6 116.3 %all-gather.3.cloned.1.call-start = ((), (), s32[]{:S(2)}) async-start(), calls=%async_computation.2 | async-start | bytes 17039360 | tf_op jit(solution)/shard_map/all_gather | solution.py:13
  36.8 380.4 %all-reduce.4.cloned.1.call-start = ((), (), s32[]{:S(2)}) async-start(), calls=%async_computation.3 | async-start | bytes 524288 | tf_op jit(solution)/shard_map/psum | solution.py:130
  235.3 292.4 %all-reduce.6.cloned.1.call-start = ((), (), s32[]{:S(2)}) async-start(), calls=%async_computation.5 | async-start | bytes 524288
  450.3 228.7 %reduce-scatter.4.cloned.1.call-start = ((), (), s32[]{:S(2)}) async-start(), calls=%async_computation.4 | async-start | bytes 2129920
Sparse Core Ops, SparseCore 0:
  36.9 100.9 all-gather.2
  235.5 181.6 all-reduce.3
  450.4 77.2 all-reduce.5
  532.3 146.7 reduce-scatter.3
where the time goes:
time: 690 us; the launch traced here: 687 us
  waiting for transfers between devices  431 us (62%)
  blocking collectives  103 us (15%)
  other arithmetic  100 us (14%)
  between operations  14.7 us (2%)
  local copies, waits for them, and re-layouts  13.4 us (2%)
  matrix products  11.9 us (2%)
  starting transfers between devices  10.5 us (2%)
    unnamed x6, waiting for transfers between devices  222 us
    psum x1, waiting for transfers between devices, shards(): projected = lax.psum(proj_terms, 'expert')  181 us
    add x63, other arithmetic, combine_parts(): out_first * factor_first[..., None] + out_second * factor_second[..., None]  91.5 us
    all_gather x2, blocking collectives, combined_all(): lax.all_gather(a.astype(kind), axis)  76.4 us
    all_gather x1, blocking collectives, shards(): piece = lax.all_gather(routed, 'dp', axis=0, tiled=True)  26.8 us
    all_gather x1, waiting for transfers between devices, combined_all(): lax.all_gather(a.astype(kind), axis)  21.4 us
  transfers between devices with their start and end apart: 5, of which 5 were waited for; matrix products, arithmetic and copies ran while one was open for 2% of the time, Pallas kernels for 0%

commit v1 on v0

--- a/solution.py
+++ b/solution.py
@@ -127,7 +127,7 @@
     ) / denominator[..., None]
     attended = attended.astype(jnp.bfloat16).reshape(local_rows, own_heads * HD)
     proj_terms = jnp.dot(attended, out_weight, preferred_element_type=jnp.float32)
-    projected = lax.psum(proj_terms, "expert")
+    projected = jnp.sum(lax.all_gather(proj_terms, "expert"), axis=0)
     stream = residual.astype(jnp.float32) + projected
     inverse = lax.rsqrt(jnp.sum(stream * stream, axis=1, keepdims=True) / model_width + 1e-06)
     normed = (stream * inverse).astype(jnp.bfloat16)

time: 690 us -> 612 us (0.89)
  waiting for transfers between devices: 431 us -> 351 us
    psum x1 -> x0, waiting for transfers between devices: 181 us -> none  [shards(): projected = lax.psum(proj_terms, 'expert')]
    all_gather x0 -> x1, waiting for transfers between devices: none -> 102 us  [shards(): projected = jnp.sum(lax.all_gather(proj_terms, 'expert'), axis=0)]
where the time goes in v1:
time: 612 us; the launch traced here: 610 us
  waiting for transfers between devices  351 us (57%)
  other arithmetic  105 us (17%)
  blocking collectives  103 us (17%)
  between operations  14.7 us (2%)
  local copies, waits for them, and re-layouts  12.7 us (2%)
  starting transfers between devices  10.5 us (2%)
  matrix products  9.78 us (2%)
    unnamed x6, waiting for transfers between devices  221 us
    all_gather x1, waiting for transfers between devices, shards(): projected = jnp.sum(lax.all_gather(proj_terms, 'expert'), axis=0)  102 us
    add x63, other arithmetic, combine_parts(): out_first * factor_first[..., None] + out_second * factor_second[..., None]  91.5 us
    all_gather x2, blocking collectives, combined_all(): lax.all_gather(a.astype(kind), axis)  76.4 us
    all_gather x1, blocking collectives, shards(): piece = lax.all_gather(routed, 'dp', axis=0, tiled=True)  26.8 us
    all_gather x1, waiting for transfers between devices, combined_all(): lax.all_gather(a.astype(kind), axis)  22.6 us
  transfers between devices with their start and end apart: 5, of which 5 were waited for; matrix products, arithmetic and copies ran while one was open for 2% of the time, Pallas kernels for 0%

profile of v1, /device:TPU:16, one launch (start us, length us, event | category | flops | bytes accessed | tf_op | source)
XLA Modules:
  0.0 609.6 jit_solution(8140369422938496428)
XLA Ops:
  11.2 10.3 %all-to-all-start = ((bf16[8,16,1024]{2,1,0:T(8,128)(2,1)}), bf16[8,16,1024]{2,1,0:T(8,128)(2,1)S(1)}, u32[]{:S(2)}, u32[]{:S(2)}) async-start(bf16[8,16,1024]{2,1,0:T(8,128)(2,1)} %broadcast_select_fusion), calls=%async_computation | async-start | bytes 524288 | tf_op jit(solution)/shard_map/all_to_all | solution.py:78
  24.8 1.7 copy.82
  27.3 6.2 %all-to-all-done = bf16[8,16,1024]{2,1,0:T(8,128)(2,1)S(1)} async-done(((bf16[8,16,1024]{2,1,0:T(8,128)(2,1)}), bf16[8,16,1024]{2,1,0:T(8,128)(2,1)S(1)}, u32[]{:S(2)}, u32[]{:S(2)}) %all-to-all-start) | async-done | bytes 262176 | tf_op jit(solution)/shard_map/all_to_all | solution.py:78
  38.8 39.2 %all_gather.23 = bf16[64,16,64]{2,1,0:T(8,128)(2,1)S(1)} all-gather(bf16[1,16,64]{2,1,0:T(8,128)(2,1)S(1)} %convert_element_type.161), channel_id=1, replica_groups=mesh['dp'=8,'expert'=64] {'expert'}, dimensions={0}, use_global_device_ids=true | all-gather | bytes 133120 | tf_op jit(solution)/shard_map/all_gather | solution.py:13
  78.1 37.2 %all_gather.22 = bf16[64,16,64]{2,1,0:T(8,128)(2,1)S(1)} all-gather(bf16[1,16,64]{2,1,0:T(8,128)(2,1)S(1)} %convert_element_type.157), channel_id=1, replica_groups=mesh['dp'=8,'expert'=64] {'expert'}, dimensions={0}, use_global_device_ids=true | all-gather | bytes 133120 | tf_op jit(solution)/shard_map/all_gather | solution.py:13
  115.3 22.6 %all-gather.5.cloned.1.call-done = bf16[64,16,64,128]{3,2,1,0:T(8,128)(2,1)} async-done(((bf16[1,16,64,128]{3,2,1,0:T(8,128)(2,1)}), bf16[64,16,64,128]{3,2,1,0:T(8,128)(2,1)}) %all-gather.5.cloned.1.call-update) | async-done | bytes 16777232 | tf_op jit(solution)/shard_map/all_gather | solution.py:13
  138.9 94.9 %while.20 = (s32[]{:T(128)}, f32[16,64,128]{2,1,0:T(8,128)S(1)}, f32[16,64]{1,0:T(8,128)S(1)}, f32[16,64]{1,0:T(8,128)S(1)}, bf16[64,16,64]{2,1,0:T(8,128)(2,1)S...) while((s32[]{:T(128)}, f32[16,64,128]{2,1,0:T(8,128)S(1)}, ...), condition=%wide.region_4.5_spmd, body=%wide.region_3.4_spmd.sunk | while | flops 532485 | bytes 1347735 | solution.py:25
  140.4 1.5 fusion.71
  143.5 1.5 fusion.71
  146.5 1.5 fusion.71
  148.0 1.5 fusion.71
  149.5 1.5 fusion.71
  151.0 1.5 fusion.71
  154.0 1.5 fusion.71
  157.0 1.5 fusion.71
  160.0 1.5 fusion.71
  163.0 1.5 fusion.71
  236.3 101.5 %all-gather.7.cloned.1.call-done = f32[1024,4096]{1,0:T(8,128)} async-done(((f32[16,4096]{1,0:T(8,128)}), f32[1024,4096]{1,0:T(8,128)}) %all-gather.7.cloned.1.call-update) | async-done | bytes 16777232 | tf_op jit(solution)/shard_map/all_gather | solution.py:130
  337.8 6.6 %reduce_sum.56 = f32[16,4096]{1,0:T(8,128)S(1)} reduce(f32[64,16,4096]{2,1,0:T(8,128)} %bitcast.98, f32[]{:T(128)} %constant.124.clone.1), dimensions={0}, to_apply=%region_6.8 | reduce | flops 4128768 | bytes 17039364 | tf_op jit(solution)/shard_map/reduce_sum | solution.py:130
  344.8 26.8 %all-gather.1 = bf16[8,4,4096]{2,1,0:T(4,128)(2,1)S(1)} all-gather(bf16[1,4,4096]{2,1,0:T(4,128)(2,1)S(1)} %fusion.3), channel_id=1, replica_groups=mesh['dp'=8,'expert'=64] {'dp'}, dimensions={0}, use_global_device_ids=true | all-gather | bytes 294912 | tf_op jit(solution)/shard_map/all_gather | solution.py:153
  371.9 2.5 convolution_convert_fusion
  376.4 73.3 %all-reduce.3.cloned.1.call-done = bf16[32,4096]{1,0:T(8,128)(2,1)} async-done(((bf16[32,4096]{1,0:T(8,128)(2,1)}), bf16[32,4096]{1,0:T(8,128)(2,1)}) %all-reduce.3.cloned.1.call-update) | async-done | bytes 262160
  449.7 3.4 convolution_bitcast_fusion
  453.8 147.8 %reduce-scatter.4.cloned.1.call-done = f32[64,16]{1,0:T(8,128)} async-done(((f32[4096,16]{1,0:T(8,128)}), f32[64,16]{1,0:T(8,128)}) %reduce-scatter.4.cloned.1.call-update) | async-done | bytes 4112
  (193 shorter events, 99.2 us)
Async XLA Ops:
  7.2 364.8 %copy-start = (bf16[1,128,4096]{2,1,0:T(8,128)(2,1)S(1)}, bf16[1,128,4096]{2,1,0:T(8,128)(2,1)}, u32[]{:S(2)}) copy-start(bf16[1,128,4096]{2,1,0:T(8,128)(2,1)} %param.31) | copy-start | bytes 3145732
  7.2 227.1 %copy-start.1 = (bf16[128,4096]{1,0:T(8,128)(2,1)S(1)}, bf16[128,4096]{1,0:T(8,128)(2,1)}, u32[]{:S(2)}) copy-start(bf16[128,4096]{1,0:T(8,128)(2,1)} %param.25) | copy-start | bytes 3145732
  7.2 228.2 %copy-start.4 = (s32[128,8]{0,1:T(8,128)S(1)}, s32[128,8]{0,1:T(8,128)}, u32[]{:S(2)}) copy-start(s32[128,8]{0,1:T(8,128)} %param.27) | copy-start | bytes 12292
  7.2 228.9 %copy-start.5 = (f32[128,8]{0,1:T(8,128)S(1)}, f32[128,8]{0,1:T(8,128)}, u32[]{:S(2)}) copy-start(f32[128,8]{0,1:T(8,128)} %param.28) | copy-start | bytes 12292
  11.2 22.2 %all-to-all-start = ((bf16[8,16,1024]{2,1,0:T(8,128)(2,1)}), bf16[8,16,1024]{2,1,0:T(8,128)(2,1)S(1)}, u32[]{:S(2)}, u32[]{:S(2)}) async-start(bf16[8,16,1024]{2,1,0:T(8,128)(2,1)} %broadcast_select_fusion), calls=%async_computation | async-start | bytes 524288 | tf_op jit(solution)/shard_map/all_to_all | solution.py:78
  21.5 116.4 %all-gather.5.cloned.1.call-start = ((), (), s32[]{:S(2)}) async-start(), calls=%async_computation.2 | async-start | bytes 17039360 | tf_op jit(solution)/shard_map/all_gather | solution.py:13
  33.5 310.9 %copy-start.3 = (bf16[16,4096]{1,0:T(8,128)(2,1)S(1)}, bf16[16,4096]{1,0:T(8,128)(2,1)}, u32[]{:S(2)}) copy-start(bf16[16,4096]{1,0:T(8,128)(2,1)} %param.26) | copy-start | bytes 393220
  36.8 301.1 %all-gather.7.cloned.1.call-start = ((), (), s32[]{:S(2)}) async-start(), calls=%async_computation.3 | async-start | bytes 17039360 | tf_op jit(solution)/shard_map/all_gather | solution.py:130
  235.3 136.3 %copy-start.2 = (bf16[1,4096,128]{2,1,0:T(8,128)(2,1)S(1)}, bf16[1,4096,128]{2,1,0:T(8,128)(2,1)}, u32[]{:S(2)}) copy-start(bf16[1,4096,128]{2,1,0:T(8,128)(2,1)} %param.29) | copy-start | bytes 3145732
  235.3 214.4 %all-reduce.3.cloned.1.call-start = ((), (), s32[]{:S(2)}) async-start(), calls=%async_computation.5 | async-start | bytes 524288
  374.4 227.2 %reduce-scatter.4.cloned.1.call-start = ((), (), s32[]{:S(2)}) async-start(), calls=%async_computation.4 | async-start | bytes 2129920
Sparse Core Ops, SparseCore 0:
  36.9 100.9 all-gather.4
  235.5 102.3 all-gather.6
  374.6 75.1 all-reduce.2
  454.9 146.6 reduce-scatter.3
